TPU v7x, 128 devices: a whole 4x4x4 slice. The times are simulated.
128 devices in a mesh: group: 8 (over y_lo, x), head: 16 (over y_hi, z, core).
Axes of the slice: x: 4, y: 4 (y_hi: 2, y_lo: 2; y = y_hi * 2 + y_lo), z: 4, core: 2. Of those that a mesh axis runs over, the one named last changes fastest.
Arguments:
- symbol_lookup_table: bfloat16 [65536, 2048], P(None, 'head'), may hold values from -6 to 6
- joined_linear_maps: float32 [5, 2048, 2048], P(None, 'group', 'head'), may hold values from -0.125 to 0.125
- feedforward_lookup_map: float32 [2048, 7168], P('group', 'head'), may hold values from -0.125 to 0.125
- timeblend_result_map: float32 [2048, 2048], P('head', 'group'), may hold values from -0.125 to 0.125
- feedforward_content_map: float32 [7168, 2048], P('head', 'group'), may hold values from -0.0625 to 0.0625
- lag_blend_coefs: float32 [8, 2048], replicated, may hold values from 0 to 1
- blend_narrowing_map: bfloat16 [2048, 160], replicated, may hold values from -0.125 to 0.125
- blend_widening_maps: bfloat16 [5, 32, 2048], replicated, may hold values from -0.59765625 to 0.59765625
- fading_narrowing_map: bfloat16 [2048, 64], replicated, may hold values from -0.125 to 0.125
- fading_widening_map: bfloat16 [64, 2048], P(None, 'head'), as said below
- initial_fading_power: float32 [2048], P('head'), may hold values from -12 to -2.9
- present_symbol_extra: float32 [2048], P('head'), may hold values from -3 to 3
- attender_scaling_coefs: float32 [2048], P('head'), may hold values from 0.5 to 2
- active_cluster_sheets: int32 [8], replicated, may hold values from 2 to 4, as said below
- sheets_for_inquiry: int32 [7], replicated, may hold values from 2 to 7, as said below
- sheet_symbol_indices: int32 [24, 256], replicated, may hold values from 0 to 65535
Outputs:
- hidden_states: bfloat16 [8192, 2048], P('group', 'head')
- page_states: float32 [32, 32, 4096], P('group', 'head')
- shift_edges: float32 [32, 2, 2048], P('group', None, 'head')
Inputs may be any that keep to these rules, and one draw needn't show every extreme that they name: `active_cluster_sheets`: they sum to 24; the two groups at one end of the axis, the first two or the last two, hold 4 pages each. `sheets_for_inquiry`: they sum to 24; the first page of every group but group 0 continues a request; the first or the last request holds 7 pages. `fading_widening_map`: each entry lies within 2.5 / sqrt(64) of zero.
All inputs are finite; a program needn't handle non-finite values.
Results may differ from a plain program's by a relative error of at most 0.017.
Values may be sent and summed in bfloat16 or wider, within the bound.
No kernel may reach another device: no remote copies, remote signals or barrier semaphores. Data moves between devices by JAX's collectives and lax.ppermute only.
A program may use at most 192 MiB of HBM per device.

v0:
```python
import jax
import jax.numpy as jnp
from jax import lax
from jax.sharding import PartitionSpec as P

ATTENTION_DEPTH = 64
PAGE = 256
SLOTS = 4
BLOCK = 128
EXACT_ARITHMETIC = lax.Precision.HIGHEST
LAYER_EPS = 1e-05
GROUP_EPS = 0.00064


def passed_along(value, axis, steps):
    count = lax.axis_size(axis)
    initial, last = (max(0, -steps), min(count, count - steps))
    return lax.ppermute(value, axis, [(source, source + steps) for source in range(initial, last)])


def layer_norm(value_rows):
    value_rows = value_rows.astype(jnp.float32)
    centered = value_rows - jnp.mean(value_rows, axis=-1, keepdims=True)
    return centered * lax.rsqrt(jnp.mean(centered * centered, axis=-1, keepdims=True) + LAYER_EPS)


def mixed_inputs(current, previous, lag_blend_coefs, blend_narrowing_map, blend_widening_maps):
    delta_rows = previous - current
    seeded = (current + delta_rows * lag_blend_coefs[0]).astype(jnp.bfloat16)
    low_rank = jnp.tanh(
        jnp.dot(seeded, blend_narrowing_map, preferred_element_type=jnp.float32)
    ).astype(jnp.bfloat16)
    rank_width = blend_widening_maps.shape[1]
    result_lines = []
    for number in range(5):
        column_part = low_rank[:, number * rank_width : (number + 1) * rank_width]
        offset = jnp.dot(
            column_part, blend_widening_maps[number], preferred_element_type=jnp.float32
        )
        result_lines.append(
            (current + delta_rows * (lag_blend_coefs[number + 1] + offset)).astype(jnp.bfloat16)
        )
    return result_lines


def log_decay(mixed_decay, fading_narrowing_map, fading_widening_map, initial_fading_power):
    hidden_low = jnp.tanh(
        jnp.dot(mixed_decay, fading_narrowing_map, preferred_element_type=jnp.float32)
    ).astype(jnp.bfloat16)
    return -jnp.exp(
        initial_fading_power
        + jnp.dot(hidden_low, fading_widening_map, preferred_element_type=jnp.float32)
    )


def group_norm(value_rows):
    shaped = value_rows.reshape(value_rows.shape[0], -1, ATTENTION_DEPTH)
    centered = shaped - jnp.mean(shaped, axis=-1, keepdims=True)
    normed = centered * lax.rsqrt(jnp.mean(centered * centered, axis=-1, keepdims=True) + GROUP_EPS)
    return normed.reshape(value_rows.shape)


def per_device(
    symbol_lookup_table,
    joined_linear_maps,
    feedforward_lookup_map,
    timeblend_result_map,
    feedforward_content_map,
    lag_blend_coefs,
    blend_narrowing_map,
    blend_widening_maps,
    fading_narrowing_map,
    fading_widening_map,
    initial_fading_power,
    present_symbol_extra,
    attender_scaling_coefs,
    active_cluster_sheets,
    sheets_for_inquiry,
    sheet_symbol_indices,
):
    group_count = lax.axis_size("group")
    group_here = lax.axis_index("group")
    head_here = lax.axis_index("head")
    features_on_shard = present_symbol_extra.shape[0]
    attenders_on_shard = features_on_shard // ATTENTION_DEPTH
    slot_rows = SLOTS * PAGE
    full_width = lag_blend_coefs.shape[1]
    group_number = jnp.arange(group_count, dtype=jnp.int32)
    pick_group = group_number == group_here
    live_count = jnp.sum(jnp.where(pick_group, active_cluster_sheets, 0))
    group_first = jnp.cumsum(active_cluster_sheets) - active_cluster_sheets
    first_page = jnp.sum(jnp.where(pick_group, group_first, 0))
    slot_number = jnp.arange(SLOTS, dtype=jnp.int32)
    slot_live = slot_number < live_count
    request_first = jnp.cumsum(sheets_for_inquiry) - sheets_for_inquiry
    page_here = first_page + slot_number
    begins = jnp.any(page_here[:, None] == request_first[None, :], axis=1)
    continues = jnp.where(slot_live & jnp.logical_not(begins), 1.0, 0.0).astype(jnp.float32)
    safe_page = jnp.where(slot_live, page_here, 0)
    tokens_here = jnp.take(sheet_symbol_indices, safe_page, axis=0)
    before_token = jnp.take(sheet_symbol_indices[:, -1], jnp.maximum(safe_page - 1, 0))
    own_rows = jnp.take(symbol_lookup_table, tokens_here.reshape(-1), axis=0)
    own_edges = jnp.take(symbol_lookup_table, before_token, axis=0)
    embedded, edge_rows = (
        lax.all_gather(own_rows, "head", axis=1, tiled=True),
        lax.all_gather(own_edges, "head", axis=1, tiled=True),
    )
    stack_half = joined_linear_maps.astype(jnp.bfloat16)
    key_half = feedforward_lookup_map.astype(jnp.bfloat16)
    output_half = timeblend_result_map.astype(jnp.bfloat16)
    value_half = feedforward_content_map.astype(jnp.bfloat16)
    projections, key_weight, output_weight, value_weight = (
        lax.all_gather(stack_half, "group", axis=1, tiled=True),
        lax.all_gather(key_half, "group", axis=0, tiled=True),
        lax.all_gather(output_half, "group", axis=1, tiled=True),
        lax.all_gather(value_half, "group", axis=1, tiled=True),
    )
    current = layer_norm(embedded)
    edge_first = layer_norm(edge_rows) * continues[:, None]
    current_pages = current.reshape(SLOTS, PAGE, full_width)
    previous = jnp.concatenate([edge_first[:, None, :], current_pages[:, :-1, :]], axis=1).reshape(
        slot_rows, full_width
    )
    mixed_decay, mixed_key, mixed_value, mixed_query, mixed_gate = mixed_inputs(
        current, previous, lag_blend_coefs, blend_narrowing_map, blend_widening_maps
    )
    fading_multipliers = log_decay(
        mixed_decay, fading_narrowing_map, fading_widening_map, initial_fading_power
    )
    acceptance_lines = jnp.dot(mixed_query, projections[0], preferred_element_type=jnp.float32)
    present_lookups = jnp.dot(mixed_key, projections[1], preferred_element_type=jnp.float32)
    present_contents = jnp.dot(mixed_value, projections[2], preferred_element_type=jnp.float32)
    gate_raw = jnp.dot(mixed_gate, projections[3], preferred_element_type=jnp.float32)
    gating = jax.nn.silu(gate_raw)
    blocks = slot_rows // BLOCK
    per_page = PAGE // BLOCK

    def to_blocks(value_rows):
        return value_rows.reshape(blocks, BLOCK, attenders_on_shard, ATTENTION_DEPTH).transpose(
            0, 2, 1, 3
        )

    block_index = jnp.arange(blocks, dtype=jnp.int32)
    block_start = block_index % per_page == 0
    block_slot = block_index // per_page
    slot_keep = continues * (slot_number > 0)
    keep_state = jnp.where(block_start, jnp.take(slot_keep, block_slot), 1.0)
    keep_factor = jnp.where(block_start, jnp.take(continues, block_slot), 1.0)
    attender_extra = present_symbol_extra.reshape(attenders_on_shard, ATTENTION_DEPTH)
    strictly_lower = jnp.arange(BLOCK)[:, None] > jnp.arange(BLOCK)[None, :]

    def decay_block(retained_memory, inputs):
        sequential_sweep, factor = retained_memory
        segment_askers, segment_lookups, value_block, decay_rows, keep_one, keep_two = inputs
        sequential_sweep = sequential_sweep * keep_one
        factor = factor * keep_two
        inclusive = jnp.cumsum(decay_rows, axis=1)
        exclusive = inclusive - decay_rows
        query_scaled = segment_askers * jnp.exp(exclusive)
        key_scaled = segment_lookups * jnp.exp(-inclusive)
        scores = jnp.einsum("hts,hus->htu", query_scaled, key_scaled, precision=EXACT_ARITHMETIC)
        scores = jnp.where(strictly_lower, scores, 0.0)
        selfpair_contribution = jnp.sum(
            segment_askers * attender_extra[:, None, :] * segment_lookups, axis=2
        )
        sublevel_result = (
            jnp.einsum("htu,huj->htj", scores, value_block, precision=EXACT_ARITHMETIC)
            + selfpair_contribution[:, :, None] * value_block
            + jnp.einsum("hts,hsj->htj", query_scaled, sequential_sweep, precision=EXACT_ARITHMETIC)
        )
        block_total = inclusive[:, -1, :]
        key_end = segment_lookups * jnp.exp(block_total[:, None, :] - inclusive)
        sequential_sweep = jnp.exp(block_total)[:, :, None] * sequential_sweep + jnp.einsum(
            "hts,htj->hsj", key_end, value_block, precision=EXACT_ARITHMETIC
        )
        carry_rows = query_scaled * factor[:, None, :]
        factor = factor * jnp.exp(block_total)
        return ((sequential_sweep, factor), (sublevel_result, carry_rows, sequential_sweep, factor))

    start_state = jnp.zeros((attenders_on_shard, ATTENTION_DEPTH, ATTENTION_DEPTH), jnp.float32)
    start_factor = jnp.ones((attenders_on_shard, ATTENTION_DEPTH), jnp.float32)
    final_carry, (block_out, carry_rows, block_states, block_factors) = lax.scan(
        decay_block,
        (start_state, start_factor),
        (
            to_blocks(acceptance_lines),
            to_blocks(present_lookups),
            to_blocks(present_contents),
            to_blocks(fading_multipliers),
            keep_state,
            keep_factor,
        ),
    )
    page_end = block_states[per_page - 1 :: per_page]
    page_factor = block_factors[per_page - 1 :: per_page]
    last_pick = (slot_number == live_count - 1).astype(jnp.float32)
    leaving_state = jnp.einsum("s,shij->hij", last_pick, page_end, precision=EXACT_ARITHMETIC)
    leaving_factor = jnp.einsum("s,shi->hi", last_pick, page_factor, precision=EXACT_ARITHMETIC)

    def relay_step(turn_number, incoming):
        return passed_along(
            (leaving_factor[:, :, None] * incoming + leaving_state).astype(jnp.bfloat16), "group", 1
        ).astype(jnp.float32)

    incoming = lax.fori_loop(0, group_count - 1, relay_step, jnp.zeros_like(leaving_state))
    block_out = block_out + jnp.einsum(
        "bhts,hsj->bhtj", carry_rows, incoming, precision=EXACT_ARITHMETIC
    )
    page_end = page_end + page_factor[:, :, :, None] * incoming[None]
    attended = block_out.transpose(0, 2, 1, 3).reshape(slot_rows, features_on_shard)
    normed = (group_norm(attended) * attender_scaling_coefs * gating).astype(jnp.bfloat16)
    mixer_total = lax.psum(
        jnp.dot(normed, output_weight, preferred_element_type=jnp.float32).astype(jnp.bfloat16),
        "head",
    ).astype(jnp.float32)
    residual = (embedded.astype(jnp.float32) + mixer_total).astype(jnp.bfloat16)
    last_residual = lax.dynamic_slice_in_dim(residual, live_count * PAGE - 1, 1, 0)
    arriving = passed_along(last_residual, "group", 1)
    channel_in = layer_norm(residual)
    channel_pages = channel_in.reshape(SLOTS, PAGE, full_width)
    edge_two = (
        jnp.concatenate([layer_norm(arriving), channel_pages[:-1, -1, :]], axis=0)
        * continues[:, None]
    )
    channel_prev = jnp.concatenate(
        [edge_two[:, None, :], channel_pages[:, :-1, :]], axis=1
    ).reshape(slot_rows, full_width)
    channel_delta = channel_prev - channel_in
    key_input = (channel_in + channel_delta * lag_blend_coefs[6]).astype(jnp.bfloat16)
    gate_input = (channel_in + channel_delta * lag_blend_coefs[7]).astype(jnp.bfloat16)
    gate_raw_two = jnp.dot(gate_input, projections[4], preferred_element_type=jnp.float32)
    key_raw = jnp.dot(key_input, key_weight, preferred_element_type=jnp.float32)
    squared = jnp.square(jax.nn.relu(key_raw)).astype(jnp.bfloat16)
    channel = lax.psum_scatter(
        jnp.dot(squared, value_weight, preferred_element_type=jnp.float32).astype(jnp.bfloat16),
        "head",
        scatter_dimension=1,
        tiled=True,
    ).astype(jnp.float32)
    gate_two = jax.nn.sigmoid(gate_raw_two)
    residual_local = lax.dynamic_slice_in_dim(
        residual, head_here * features_on_shard, features_on_shard, 1
    )
    hidden = (residual_local.astype(jnp.float32) + gate_two * channel).astype(jnp.bfloat16)
    row_live = jnp.repeat(slot_live, PAGE)
    hidden_out = jnp.where(row_live[:, None], hidden, jnp.zeros_like(hidden))
    state_out = page_end.reshape(SLOTS, attenders_on_shard, ATTENTION_DEPTH * ATTENTION_DEPTH)
    state_out = jnp.where(slot_live[:, None, None], state_out, jnp.zeros_like(state_out))
    first_edge = lax.dynamic_slice_in_dim(
        current_pages[:, -1, :], head_here * features_on_shard, features_on_shard, 1
    )
    second_edge = lax.dynamic_slice_in_dim(
        channel_pages[:, -1, :], head_here * features_on_shard, features_on_shard, 1
    )
    edge_out = jnp.stack([first_edge, second_edge], axis=1)
    edge_out = jnp.where(slot_live[:, None, None], edge_out, jnp.zeros_like(edge_out))
    return (hidden_out, state_out, edge_out)


def solution(mesh):
    in_specs = (
        P(None, "head"),
        P(None, "group", "head"),
        P("group", "head"),
        P("head", "group"),
        P("head", "group"),
        P(),
        P(),
        P(),
        P(),
        P(None, "head"),
        P("head"),
        P("head"),
        P("head"),
        P(),
        P(),
        P(),
    )
    out_specs = (P("group", "head"), P("group", "head", None), P("group", None, "head"))
    return jax.shard_map(
        per_device, mesh=mesh, in_specs=in_specs, out_specs=out_specs, check_vma=False
    )
```

profile of v0, /device:TPU:0, one launch (start us, length us, event | category | flops | bytes accessed | tf_op | source)
XLA Modules:
  0.0 668.3 jit_solution(10876387743382121126)
XLA Ops:
  7.2 1.9 convert_element_type.97
  15.4 10.8 %gather_fusion.1 = bf16[1024,128]{1,0:T(8,128)(2,1)S(1)} fusion(bf16[65536,128]{1,0:T(8,128)(2,1)} %param.22, s32[1024]{0:T(1024)S(1)} %broadcast_clamp_fusion), kind=kCustom, calls=%fused_computation.3 | custom fusion | bytes 528384 | tf_op jit(solution)/shard_map/jit(_take)/gather | solution.py:102
  36.4 8.6 %gather_fusion.3 = bf16[4,128]{1,0:T(4,128)(2,1)S(1)} fusion(bf16[65536,128]{1,0:T(8,128)(2,1)} %param.22, s32[1024]{0:T(1024)S(1)} %pad_clamp_fusion.1), kind=kCustom, calls=%fused_computation.5 | custom fusion | bytes 2064 | tf_op jit(solution)/shard_map/jit(_take)/gather | solution.py:103
  46.5 25.8 %all_gather.19 = bf16[4,2048]{1,0:T(4,128)(2,1)S(1)} all-gather(bf16[4,128]{1,0:T(4,128)(2,1)S(1)} %broadcast_select_fusion.2), channel_id=1, replica_groups=mesh['group'=8,'head'=16] {'head'}, dimensions={1}, use_global_device_ids=true | all-gather | bytes 17408 | tf_op jit(solution)/shard_map/all_gather | solution.py:106
  73.7 29.2 %all_gather.21 = bf16[128,2048]{1,0:T(8,128)(2,1)S(1)} all-gather(bf16[128,256]{1,0:T(8,128)(2,1)S(1)} %convert_element_type.102), channel_id=1, replica_groups=mesh['group'=8,'head'=16] {'group'}, dimensions={1}, use_global_device_ids=true | all-gather | bytes 589824 | tf_op jit(solution)/shard_map/all_gather | solution.py:115
  104.2 2.3 slice_bitcast_fusion.4
  108.2 6.0 all-gather.5.cloned.1.call-done
  114.1 3.0 convert_reduce_fusion
  117.1 3.4 fusion.32
  121.5 4.7 pad_maximum_fusion
  127.2 4.7 bitcast_subtract_fusion.2
  131.9 2.7 fusion.49
  135.1 8.0 %fusion.56 = bf16[1024,64]{0,1:T(8,128)(2,1)S(1)} fusion(bf16[2048,64]{0,1:T(8,128)(2,1)} %param.30, f32[1024,2048]{1,0:T(8,128)} %copy-done.4, bf16[1024,2048]{1,0:T(8,128)(2,1)} %all-gather.5.cloned.1.call-done, f32[2048]{0:T(1024)S(1)} %bitcast.323, f32[1024]{0:T(1024)S(1)} %add_rsqrt_fusion.1, f32[1024]{0:T(1024)S(1)} %broadcast_multiply_fusion.2, ...), kind=kOutput, calls=%fused_computation.107 | convolution fusion | flops 417398784 | bytes 13189120 | tf_op jit(solution)/shard_map/dot_general | solution.py:48
  144.4 1.9 copy.138
  146.4 6.0 add_convert_fusion.3
  152.4 2.4 convolution_bitcast_fusion.1
  154.8 3.6 add_convert_fusion.4
  159.9 3.6 add_convert_fusion.5
  165.0 74.7 %while.32 = (s32[]{:T(128)}, f32[2,64,64]{2,1,0:T(8,128)S(1)}, f32[2,64]{1,0:T(2,128)S(1)}, f32[8,2,128,64]{2,3,0,1:T(8,128)}, f32[8,2,128,64]{3,2,0,1:T(8,128)}...) while((s32[]{:T(128)}, f32[2,64,64]{2,1,0:T(8,128)S(1)}, ...), condition=%wide.region_12.14_spmd.clone, body=%wide.region_9.13_spmd.clone.sunk | while | flops 77955200 | bytes 2999012 | solution.py:182
  198.5 1.7 fusion.134
  200.1 1.7 bitcast_dynamic-update-slice_fusion.4
  209.4 1.7 bitcast_dynamic-update-slice_fusion.4
  217.1 1.7 fusion.134
  226.4 1.7 fusion.134
  228.1 1.7 bitcast_dynamic-update-slice_fusion.4
  241.4 43.2 %while.33 = (s32[]{:T(128)}, f32[2,64,64]{2,1,0:T(8,128)S(1)}, f32[2,64]{1,0:T(2,128)S(1)}, f32[2,64,64]{2,1,0:T(8,128)S(1)}, s32[]{:T(128)}, /*index=5*/s32[]{:T(128)}) while((s32[]{:T(128)}, f32[2,64,64]{2,1,0:T(8,128)S(1)}, f32[2,64]{1,0:T(2,128)S(1)}, f32[2,64,64]{2,1,0:T(8,128)S(1)}, s32[]{:T(128)}, ...), condition=%wide.region_14.16_spmd.clone, body=%wide.region_13.15_spmd.clone.sunk | while | flops 40963 | bytes 197239 | solution.py:205
  241.5 2.2 collective-permute-start
  245.4 4.2 collective-permute-start
  251.3 4.2 collective-permute-start
  257.2 4.2 collective-permute-start
  263.1 4.2 collective-permute-start
  269.0 6.0 collective-permute-start
  276.7 6.3 collective-permute-start
  284.6 2.7 fusion.109
  289.9 7.7 %multiply_convert_fusion.1 = bf16[1024,128]{1,0:T(8,128)(2,1)S(1)} fusion(bf16[5,2048,128]{2,1,0:T(8,128)(2,1)} %all-gather.7.cloned.1.call-done, f32[1024,2048]{1,0:T(8,128)} %copy-done.4, bf16[1024,2048]{1,0:T(8,128)(2,1)} %all-gather.5.cloned.1.call-done, f32[2048]{0:T(1024)S(1)} %bitcast.322, f32[1024]{0:T(1024)S(1)} %add_rsqrt_fusion.1, ...), kind=kOutput, calls=%fused_computation.114 | convolution fusion | flops 686948352 | bytes 15155712 | tf_op jit(solution)/shard_map/dot_general | solution.py:133
  297.6 3.2 convolution_convert_fusion.1
  303.1 156.8 %all-reduce.2.cloned.1.call-done = bf16[1024,2048]{1,0:T(8,128)(2,1)} async-done(((bf16[1024,2048]{1,0:T(8,128)(2,1)}), bf16[1024,2048]{1,0:T(8,128)(2,1)}) %all-reduce.2.cloned.1.call-update) | async-done | bytes 4194320 | tf_op jit(solution)/shard_map/psum | solution.py:212
  459.9 4.8 convert_reduce_fusion.1
  466.0 3.6 collective-permute-start.1
  470.5 3.2 copy-done.7
  476.4 4.7 pad_maximum_fusion.1
  481.1 4.5 bitcast_subtract_fusion.1
  485.6 18.9 %all-gather.9.cloned.1.call-done = bf16[2048,448]{0,1:T(8,128)(2,1)} async-done(((bf16[256,448]{0,1:T(8,128)(2,1)}), bf16[2048,448]{0,1:T(8,128)(2,1)}) %all-gather.9.cloned.1.call-update) | async-done | bytes 1835024 | tf_op jit(solution)/shard_map/all_gather | solution.py:114
  504.6 46.5 %all-gather.11.cloned.1.call-done = bf16[448,2048]{1,0:T(8,128)(2,1)} async-done(((bf16[448,256]{1,0:T(8,128)(2,1)}), bf16[448,2048]{1,0:T(8,128)(2,1)}) %all-gather.11.cloned.1.call-update) | async-done | bytes 1835024 | tf_op jit(solution)/shard_map/all_gather | solution.py:116
  551.1 12.2 %convolution_convert_fusion = bf16[1024,2048]{1,0:T(8,128)(2,1)} fusion(bf16[448,2048]{1,0:T(8,128)(2,1)} %all-gather.11.cloned.1.call-done, bf16[2048,448]{0,1:T(8,128)(2,1)} %all-gather.9.cloned.1.call-done, f32[1024,2048]{1,0:T(8,128)} %bitcast_subtract_fusion.1, f32[2048]{0:T(1024)S(1)} %bitcast.321, bf16[1024,2048]{1,0:T(8,128)(2,1)} %copy-done.5, ...), kind=kOutput, calls=%fused_computation.83 | convolution fusion | flops 3774152704 | bytes 20463616 | tf_op jit(solution)/shard_map/dot_general | solution.py:235
  563.3 6.5 copy.116
  574.3 78.4 %reduce-scatter.4.cloned.1.call-done = bf16[128,1024]{1,0:T(8,128)(2,1)} async-done(((bf16[2048,1024]{1,0:T(8,128)(2,1)}), bf16[128,1024]{1,0:T(8,128)(2,1)}) %reduce-scatter.4.cloned.1.call-update) | async-done | bytes 262160
  653.9 7.3 %fusion.57 = bf16[1024,128]{1,0:T(8,128)(2,1)} fusion(f32[1024,2048]{1,0:T(8,128)} %bitcast_subtract_fusion.1, f32[2048]{0:T(1024)S(1)} %bitcast.320, bf16[5,2048,128]{2,1,0:T(8,128)(2,1)} %all-gather.7.cloned.1.call-done, bf16[1024,128]{1,0:T(8,128)(2,1)S(1)} %copy.117, bf16[1024,2048]{1,0:T(8,128)(2,1)} %copy-done.5, s32[]{:T(128)S(6)} %select_n.209, ...), kind=kOutput, calls=%fused_computation.108 | convolution fusion | flops 550633472 | bytes 13911044 | tf_op jit(solution)/shard_map/dot_general | solution.py:231
  (314 shorter events, 119.1 us)
Async XLA Ops:
  7.2 124.7 %copy-start = (bf16[2048,160]{0,1:T(8,128)(2,1)S(1)}, bf16[2048,160]{0,1:T(8,128)(2,1)}, u32[]{:S(2)}) copy-start(bf16[2048,160]{0,1:T(8,128)(2,1)} %param.28) | copy-start | bytes 1966084
  7.2 97.0 %all-gather.7.cloned.1.call-start = ((), (), s32[]{:S(2)}) async-start(), calls=%async_computation.2 | async-start | bytes 2949120 | tf_op jit(solution)/shard_map/all_gather | solution.py:113
  9.2 105.0 %all-gather.5.cloned.1.call-start = ((), (), s32[]{:S(2)}) async-start(), calls=%async_computation.1 | async-start | bytes 4456448 | tf_op jit(solution)/shard_map/all_gather | solution.py:105
  27.2 432.7 %all-reduce.2.cloned.1.call-start = ((), (), s32[]{:S(2)}) async-start(), calls=%async_computation.3 | async-start | bytes 8388608 | tf_op jit(solution)/shard_map/psum | solution.py:212
  114.1 6.4 copy-start.2
  121.5 5.7 copy-start.8
  131.8 3.2 copy-start.4
  135.1 24.8 %copy-start.12 = (bf16[1024,160]{0,1:T(8,128)(2,1)}, bf16[1024,160]{0,1:T(8,128)(2,1)S(1)}, u32[]{:S(2)}) copy-start(bf16[1024,160]{0,1:T(8,128)(2,1)S(1)} %fusion.49) | copy-start | bytes 983044
  135.1 8.0 %copy-start.13 = (bf16[64,128]{1,0:T(8,128)(2,1)S(1)}, bf16[64,128]{1,0:T(8,128)(2,1)}, u32[]{:S(2)}) copy-start(bf16[64,128]{1,0:T(8,128)(2,1)} %param.31) | copy-start | bytes 49156
  135.1 8.0 %copy-start.14 = (f32[128]{0:T(128)S(1)}, f32[128]{0:T(128)}, u32[]{:S(2)}) copy-start(f32[128]{0:T(128)} %param.32) | copy-start | bytes 1540
  146.4 8.4 %slice-start = ((s8[8388608]{0:T(1024)(128)(4,1)}), s8[4194304]{0:T(1024)(128)(4,1)S(1)}, s32[]{:S(2)}) async-start(s8[8388608]{0:T(1024)(128)(4,1)} %bitcast.287), calls=%async_computation.7 | async-start | bytes 8388608
  146.4 8.4 %copy-start.3 = (bf16[1024,2048]{1,0:T(8,128)(2,1)S(1)}, bf16[1024,2048]{1,0:T(8,128)(2,1)}, u32[]{:S(2)}) copy-start(bf16[1024,2048]{1,0:T(8,128)(2,1)} %all-gather.5.cloned.1.call-done) | copy-start | bytes 12582916
  146.4 8.4 %slice-start.1 = ((s8[8388608]{0:T(1024)(128)(4,1)}), s8[4194304]{0:T(1024)(128)(4,1)S(1)}, s32[]{:S(2)}) async-start(s8[8388608]{0:T(1024)(128)(4,1)} %bitcast.287), calls=%async_computation.8 | async-start | bytes 8388608
  159.9 5.1 copy-start.15
  239.8 50.1 %copy-start.16 = (f32[128]{0:T(128)S(1)}, f32[128]{0:T(128)}, u32[]{:S(2)}) copy-start(f32[128]{0:T(128)} %param.34) | copy-start | bytes 1540
  241.5 3.8 collective-permute-start
  245.4 5.8 collective-permute-start
  251.3 5.8 collective-permute-start
  257.2 5.8 collective-permute-start
  263.1 5.8 collective-permute-start
  269.0 7.6 %collective-permute-start = (bf16[2,64,64]{2,1,0:T(8,128)(2,1)S(1)}, bf16[2,64,64]{2,1,0:T(8,128)(2,1)S(1)}, u32[]{:S(2)}, u32[]{:S(2)}) collective-permute-start(bf16[2,64,64]{2,1,0:T(8,128)(2,1)S(1)} %fusion.135), channel_id=1, source_target_pairs={{0,16},{16,32},{32,48},{48,64},{64,80},{80,96},{96,112},{1,17},{17... | collective-permute-start | bytes 49160 | tf_op jit(solution)/shard_map/while/body/eval_jaxpr/ppermute | solution.py:18
  276.7 7.9 %collective-permute-start = (bf16[2,64,64]{2,1,0:T(8,128)(2,1)S(1)}, bf16[2,64,64]{2,1,0:T(8,128)(2,1)S(1)}, u32[]{:S(2)}, u32[]{:S(2)}) collective-permute-start(bf16[2,64,64]{2,1,0:T(8,128)(2,1)S(1)} %fusion.135), channel_id=1, source_target_pairs={{0,16},{16,32},{32,48},{48,64},{64,80},{80,96},{96,112},{1,17},{17... | collective-permute-start | bytes 49160 | tf_op jit(solution)/shard_map/while/body/eval_jaxpr/ppermute | solution.py:18
  297.6 3.3 copy-start.10
  297.6 4.1 copy-start.11
  300.8 203.8 %all-gather.9.cloned.1.call-start = ((), (), s32[]{:S(2)}) async-start(), calls=%async_computation.4 | async-start | bytes 2064384 | tf_op jit(solution)/shard_map/all_gather | solution.py:114
  301.6 249.5 %all-gather.11.cloned.1.call-start = ((), (), s32[]{:S(2)}) async-start(), calls=%async_computation.5 | async-start | bytes 2064384 | tf_op jit(solution)/shard_map/all_gather | solution.py:116
  302.4 350.3 %reduce-scatter.4.cloned.1.call-start = ((), (), s32[]{:S(2)}) async-start(), calls=%async_computation.6 | async-start | bytes 4456448
  464.7 5.8 copy-start.5
  466.0 7.8 %collective-permute-start.1 = (bf16[1,2048]{1,0:T(2,128)(2,1)S(1)}, bf16[1,2048]{1,0:T(2,128)(2,1)S(1)}, u32[]{:S(2)}, u32[]{:S(2)}) collective-permute-start(bf16[1,2048]{1,0:T(2,128)(2,1)S(1)} %constant_dynamic-slice_fusion.5), channel_id=1, source_target_pairs={{0,16},{16,32},{32,48},{48,64},{64,80},{80,96},{96,112},{1,17},{17... | collective-permute-start | bytes 12296 | tf_op jit(solution)/shard_map/ppermute | solution.py:18
  470.5 3.2 copy-start.7
  476.4 4.7 copy-start.6
  563.3 8.2 %copy-start.9 = (f32[8,2,64,64]{3,2,1,0:T(8,128)S(1)}, f32[8,2,64,64]{3,2,1,0:T(8,128)}, u32[]{:S(2)}) copy-start(f32[8,2,64,64]{3,2,1,0:T(8,128)} %get-tuple-element.108) | copy-start | bytes 786436
  652.7 8.5 %copy-start.1 = (bf16[2048,160]{0,1:T(8,128)(2,1)S(1)}, bf16[2048,160]{0,1:T(8,128)(2,1)}, u32[]{:S(2)}) copy-start(bf16[2048,160]{0,1:T(8,128)(2,1)} %param.28) | copy-start | bytes 1966084
Sparse Core Ops, SparseCore 0:
  9.6 43.9 all-gather.6
  56.5 57.5 all-gather.4
  300.9 158.9 all-reduce.1
  461.3 43.1 all-gather.8
  506.6 44.4 all-gather.10
  569.9 82.7 reduce-scatter.3
where the time goes:
time: 678 us; the launch traced here: 668 us
  waiting for transfers between devices  318 us (47%)
  matrix products  96 us (14%)
  local copies, waits for them, and re-layouts  78.1 us (12%)
  other arithmetic  67.8 us (10%)
  blocking collectives  55 us (8%)
  starting transfers between devices  35.3 us (5%)
  between operations  17.7 us (3%)
    psum x1, waiting for transfers between devices, per_device(): lax.psum(jnp.dot(normed, output_weight, preferred_element_type=jnp.float3...  157 us
    unnamed x7, waiting for transfers between devices  78.5 us
    all_gather x1, waiting for transfers between devices, per_device(): lax.all_gather(value_half, 'group', axis=1, tiled=True)  46.5 us
    ppermute x8, starting transfers between devices, passed_along(): lax.ppermute(value, axis, [(source, source + steps) for source in range(i...  35 us
    all_gather x1, blocking collectives, per_device(): lax.all_gather(output_half, 'group', axis=1, tiled=True)  29.2 us
    dynamic_slice x56, local copies, waits for them, and re-layouts, per_device(): lax.scan(decay_block, (start_state, start_factor), (to_blocks(acceptance_...  27.3 us
    all_gather x1, blocking collectives, per_device(): lax.all_gather(own_edges, 'head', axis=1, tiled=True)  25.8 us
    all_gather x1, waiting for transfers between devices, per_device(): lax.all_gather(key_half, 'group', axis=0, tiled=True)  18.9 us
  transfers between devices with their start and end apart: 14, of which 12 were waited for; matrix products, arithmetic and copies ran while one was open for 10% of the time, Pallas kernels for 0%

commit v1 on v0

--- a/solution.py
+++ b/solution.py
@@ -113,7 +113,9 @@
         lax.all_gather(stack_half, "group", axis=1, tiled=True),
         lax.all_gather(key_half, "group", axis=0, tiled=True),
         lax.all_gather(output_half, "group", axis=1, tiled=True),
-        lax.all_gather(value_half, "group", axis=1, tiled=True),
+        jnp.concatenate(
+            lax.all_to_all(jnp.stack([value_half] * lax.axis_size("group")), "group", 0, 0), axis=1
+        ),
     )
     current = layer_norm(embedded)
     edge_first = layer_norm(edge_rows) * continues[:, None]

time: 678 us -> 629 us (0.928)
  waiting for transfers between devices: 318 us -> 264 us
  starting transfers between devices: 35.3 us -> 49.8 us
    all_gather x1 -> x0, waiting for transfers between devices: 46.5 us -> none  [per_device(): lax.all_gather(value_half, 'group', axis=1, tiled=True)]
    psum x1, waiting for transfers between devices: 157 us -> 134 us  [per_device(): lax.psum(jnp.dot(normed, output_weight, preferred_element_type=jnp.float3...]
    all_to_all x0 -> x1, waiting for transfers between devices: none -> 16 us  [per_device(): lax.all_to_all(jnp.stack([value_half] * lax.axis_size('group')), 'group',...]
    all_to_all x0 -> x1, starting transfers between devices: none -> 14.9 us  [per_device(): lax.all_to_all(jnp.stack([value_half] * lax.axis_size('group')), 'group',...]
    unnamed x45 -> x57, local copies, waits for them, and re-layouts: 14.5 us -> 15.4 us
    unnamed x7 -> x6, waiting for transfers between devices: 78.5 us -> 78.5 us
  transfers between devices with their start and end apart: 14 -> 14, of which waited for: 12 -> 12; matrix products, arithmetic and copies ran while one was open for 10% -> 11% of each run, Pallas kernels for 0% -> 0%
where the time goes in v1:
time: 629 us; the launch traced here: 620 us
  waiting for transfers between devices  264 us (42%)
  matrix products  94.5 us (15%)
  local copies, waits for them, and re-layouts  75.8 us (12%)
  other arithmetic  62.1 us (10%)
  blocking collectives  55 us (9%)
  starting transfers between devices  49.8 us (8%)
  between operations  17.5 us (3%)
    psum x1, waiting for transfers between devices, per_device(): lax.psum(jnp.dot(normed, output_weight, preferred_element_type=jnp.float3...  134 us
    unnamed x6, waiting for transfers between devices  78.5 us
    ppermute x8, starting transfers between devices, passed_along(): lax.ppermute(value, axis, [(source, source + steps) for source in range(i...  34.8 us
    all_gather x1, blocking collectives, per_device(): lax.all_gather(output_half, 'group', axis=1, tiled=True)  29.2 us
    all_gather x1, blocking collectives, per_device(): lax.all_gather(own_edges, 'head', axis=1, tiled=True)  25.8 us
    dynamic_slice x56, local copies, waits for them, and re-layouts, per_device(): lax.scan(decay_block, (start_state, start_factor), (to_blocks(acceptance_...  20.5 us
    all_gather x1, waiting for transfers between devices, per_device(): lax.all_gather(key_half, 'group', axis=0, tiled=True)  19.4 us
    all_to_all x1, waiting for transfers between devices, per_device(): lax.all_to_all(jnp.stack([value_half] * lax.axis_size('group')), 'group',...  16 us
  transfers between devices with their start and end apart: 14, of which 12 were waited for; matrix products, arithmetic and copies ran while one was open for 11% of the time, Pallas kernels for 0%

profile of v1, /device:TPU:0, one launch (start us, length us, event | category | flops | bytes accessed | tf_op | source)
XLA Modules:
  0.0 619.6 jit_solution(9119589961716809031)
XLA Ops:
  7.2 1.9 convert_element_type.97
  15.4 10.9 %gather_fusion.1 = bf16[1024,128]{1,0:T(8,128)(2,1)S(1)} fusion(bf16[65536,128]{1,0:T(8,128)(2,1)} %param.22, s32[1024]{0:T(1024)S(1)} %broadcast_clamp_fusion), kind=kCustom, calls=%fused_computation.3 | custom fusion | bytes 528384 | tf_op jit(solution)/shard_map/jit(_take)/gather | solution.py:102
  36.5 8.6 %gather_fusion.3 = bf16[4,128]{1,0:T(4,128)(2,1)S(1)} fusion(bf16[65536,128]{1,0:T(8,128)(2,1)} %param.22, s32[1024]{0:T(1024)S(1)} %pad_clamp_fusion.1), kind=kCustom, calls=%fused_computation.5 | custom fusion | bytes 2064 | tf_op jit(solution)/shard_map/jit(_take)/gather | solution.py:103
  46.5 25.8 %all_gather.16 = bf16[4,2048]{1,0:T(4,128)(2,1)S(1)} all-gather(bf16[4,128]{1,0:T(4,128)(2,1)S(1)} %broadcast_select_fusion.2), channel_id=1, replica_groups=mesh['group'=8,'head'=16] {'head'}, dimensions={1}, use_global_device_ids=true | all-gather | bytes 17408 | tf_op jit(solution)/shard_map/all_gather | solution.py:106
  73.7 29.2 %all_gather.18 = bf16[128,2048]{1,0:T(8,128)(2,1)S(1)} all-gather(bf16[128,256]{1,0:T(8,128)(2,1)S(1)} %convert_element_type.102), channel_id=1, replica_groups=mesh['group'=8,'head'=16] {'group'}, dimensions={1}, use_global_device_ids=true | all-gather | bytes 589824 | tf_op jit(solution)/shard_map/all_gather | solution.py:115
  108.8 5.7 all-gather.4.cloned.1.call-done
  114.4 3.0 convert_reduce_fusion
  117.4 3.4 fusion.32
  121.8 1.9 pad_maximum_fusion
  123.7 2.2 copy-done.8
  125.8 2.5 bitcast_subtract_fusion.2
  128.4 2.5 fusion.49
  131.6 8.0 %fusion.56 = bf16[1024,64]{0,1:T(8,128)(2,1)S(1)} fusion(bf16[2048,64]{0,1:T(8,128)(2,1)S(1)} %copy-done.20, f32[1024,2048]{1,0:T(8,128)} %copy-done.4, bf16[1024,2048]{1,0:T(8,128)(2,1)} %all-gather.4.cloned.1.call-done, f32[2048]{0:T(1024)S(1)} %bitcast.328, f32[1024]{0:T(1024)S(1)} %add_rsqrt_fusion.1, f32[1024]{0:T(1024)S(1)} %broadcast_multiply_fusion.2, ...), kind=kOutput, calls=%fused_computation.107 | convolution fusion | flops 417398784 | bytes 13189120 | tf_op jit(solution)/shard_map/dot_general | solution.py:48
  141.0 6.1 add_convert_fusion.3
  149.5 3.4 add_convert_fusion.4
  154.4 3.6 add_convert_fusion.5
  159.5 67.9 %while.32 = (s32[]{:T(128)}, f32[2,64,64]{2,1,0:T(8,128)S(1)}, f32[2,64]{1,0:T(2,128)S(1)}, f32[8,2,128,64]{2,3,0,1:T(8,128)}, f32[8,2,128,64]{3,2,0,1:T(8,128)}...) while((s32[]{:T(128)}, f32[2,64,64]{2,1,0:T(8,128)S(1)}, ...), condition=%wide.region_12.14_spmd.clone, body=%wide.region_9.13_spmd.clone.sunk | while | flops 77955200 | bytes 2999012 | solution.py:184
  165.6 1.7 bitcast_dynamic-update-slice_fusion.4
  172.5 1.7 fusion.134
  174.1 1.7 bitcast_dynamic-update-slice_fusion.4
  189.4 1.7 fusion.134
  191.1 1.7 bitcast_dynamic-update-slice_fusion.4
  199.6 1.7 bitcast_dynamic-update-slice_fusion.4
  216.5 1.7 bitcast_dynamic-update-slice_fusion.4
  229.0 43.0 %while.33 = (s32[]{:T(128)}, f32[2,64,64]{2,1,0:T(8,128)S(1)}, f32[2,64]{1,0:T(2,128)S(1)}, f32[2,64,64]{2,1,0:T(8,128)S(1)}, s32[]{:T(128)}, /*index=5*/s32[]{:T(128)}) while((s32[]{:T(128)}, f32[2,64,64]{2,1,0:T(8,128)S(1)}, f32[2,64]{1,0:T(2,128)S(1)}, f32[2,64,64]{2,1,0:T(8,128)S(1)}, s32[]{:T(128)}, ...), condition=%wide.region_14.16_spmd.clone, body=%wide.region_13.15_spmd.clone.sunk | while | flops 40963 | bytes 197239 | solution.py:207
  229.1 2.1 collective-permute-start
  232.9 4.2 collective-permute-start
  238.8 4.2 collective-permute-start
  244.7 4.2 collective-permute-start
  250.6 4.2 collective-permute-start
  256.5 5.9 collective-permute-start
  264.0 6.3 %collective-permute-start = (bf16[2,64,64]{2,1,0:T(8,128)(2,1)S(1)}, bf16[2,64,64]{2,1,0:T(8,128)(2,1)S(1)}, u32[]{:S(2)}, u32[]{:S(2)}) collective-permute-start(bf16[2,64,64]{2,1,0:T(8,128)(2,1)S(1)} %fusion.135), channel_id=1, source_target_pairs={{0,16},{16,32},{32,48},{48,64},{64,80},{80,96},{96,112},{1,17},{17... | collective-permute-start | bytes 49160 | tf_op jit(solution)/shard_map/while/body/eval_jaxpr/ppermute | solution.py:18
  272.0 2.6 fusion.109
  278.1 7.8 %multiply_convert_fusion.1 = bf16[1024,128]{1,0:T(8,128)(2,1)S(1)} fusion(bf16[5,2048,128]{2,1,0:T(8,128)(2,1)} %all-gather.6.cloned.1.call-done, f32[1024,2048]{1,0:T(8,128)} %copy-done.4, bf16[1024,2048]{1,0:T(8,128)(2,1)} %all-gather.4.cloned.1.call-done, f32[2048]{0:T(1024)S(1)} %bitcast.327, f32[1024]{0:T(1024)S(1)} %add_rsqrt_fusion.1, ...), kind=kOutput, calls=%fused_computation.114 | convolution fusion | flops 686948352 | bytes 15155712 | tf_op jit(solution)/shard_map/dot_general | solution.py:135
  285.9 3.2 convolution_convert_fusion.1
  290.5 14.9 %all-to-all-start = ((bf16[8,448,256]{2,1,0:T(8,128)(2,1)}), bf16[8,448,256]{2,1,0:T(8,128)(2,1)S(1)}, u32[]{:S(2)}, u32[]{:S(2)}) async-start(bf16[8,448,256]{2,1,0:T(8,128)(2,1)} %stack.4), calls=%async_computation | async-start | bytes 3670016 | tf_op jit(solution)/shard_map/all_to_all | solution.py:117
  306.9 16.0 %all-to-all-done = bf16[8,448,256]{2,1,0:T(8,128)(2,1)S(1)} async-done(((bf16[8,448,256]{2,1,0:T(8,128)(2,1)}), bf16[8,448,256]{2,1,0:T(8,128)(2,1)S(1)}, u32[]{:S(2)}, u32[]{:S(2)}) %all-to-all-start) | async-done | bytes 1835040 | tf_op jit(solution)/shard_map/all_to_all | solution.py:117
  324.4 133.7 %all-reduce.2.cloned.1.call-done = bf16[1024,2048]{1,0:T(8,128)(2,1)} async-done(((bf16[1024,2048]{1,0:T(8,128)(2,1)}), bf16[1024,2048]{1,0:T(8,128)(2,1)}) %all-reduce.2.cloned.1.call-update) | async-done | bytes 4194320 | tf_op jit(solution)/shard_map/psum | solution.py:214
  458.1 4.8 convert_reduce_fusion.1
  464.1 3.6 collective-permute-start.1
  468.7 3.2 copy-done.7
  474.6 4.7 pad_maximum_fusion.1
  479.3 4.5 bitcast_subtract_fusion.1
  483.8 19.4 %all-gather.8.cloned.1.call-done = bf16[2048,448]{0,1:T(8,128)(2,1)} async-done(((bf16[256,448]{0,1:T(8,128)(2,1)}), bf16[2048,448]{0,1:T(8,128)(2,1)}) %all-gather.8.cloned.1.call-update) | async-done | bytes 1835024 | tf_op jit(solution)/shard_map/all_gather | solution.py:114
  503.2 11.7 %convolution_convert_fusion = bf16[1024,2048]{1,0:T(8,128)(2,1)} fusion(bf16[448,2048]{1,0:T(8,128)(2,1)S(1)} %bitcast.310, bf16[2048,448]{0,1:T(8,128)(2,1)} %all-gather.8.cloned.1.call-done, f32[1024,2048]{1,0:T(8,128)} %bitcast_subtract_fusion.1, f32[2048]{0:T(1024)S(1)} %bitcast.326, bf16[1024,2048]{1,0:T(8,128)(2,1)} %copy-done.5, ...), kind=kOutput, calls=%fused_computation.83 | convolution fusion | flops 3774152704 | bytes 20463616 | tf_op jit(solution)/shard_map/dot_general | solution.py:237
  515.0 6.5 %copy.118 = bf16[1024,2048]{0,1:T(8,128)(2,1)} copy(bf16[1024,2048]{1,0:T(8,128)(2,1)} %convolution_convert_fusion) | data formatting | bytes 8388608
  526.0 78.4 %reduce-scatter.4.cloned.1.call-done = bf16[128,1024]{1,0:T(8,128)(2,1)} async-done(((bf16[2048,1024]{1,0:T(8,128)(2,1)}), bf16[128,1024]{1,0:T(8,128)(2,1)}) %reduce-scatter.4.cloned.1.call-update) | async-done | bytes 262160
  605.6 7.3 %fusion.57 = bf16[1024,128]{1,0:T(8,128)(2,1)} fusion(f32[1024,2048]{1,0:T(8,128)} %bitcast_subtract_fusion.1, f32[2048]{0:T(1024)S(1)} %bitcast.325, bf16[5,2048,128]{2,1,0:T(8,128)(2,1)} %all-gather.6.cloned.1.call-done, bf16[1024,128]{1,0:T(8,128)(2,1)S(1)} %copy.119, bf16[1024,2048]{1,0:T(8,128)(2,1)} %copy-done.5, s32[]{:T(128)S(6)} %select_n.209, ...), kind=kOutput, calls=%fused_computation.108 | convolution fusion | flops 550633472 | bytes 13911044 | tf_op jit(solution)/shard_map/dot_general | solution.py:233
  (327 shorter events, 117.9 us)
Async XLA Ops:
  7.2 121.2 %copy-start = (bf16[2048,160]{0,1:T(8,128)(2,1)S(1)}, bf16[2048,160]{0,1:T(8,128)(2,1)}, u32[]{:S(2)}) copy-start(bf16[2048,160]{0,1:T(8,128)(2,1)} %param.28) | copy-start | bytes 1966084
  7.2 97.0 %all-gather.6.cloned.1.call-start = ((), (), s32[]{:S(2)}) async-start(), calls=%async_computation.3 | async-start | bytes 2949120 | tf_op jit(solution)/shard_map/all_gather | solution.py:113
  9.2 105.3 %all-gather.4.cloned.1.call-start = ((), (), s32[]{:S(2)}) async-start(), calls=%async_computation.2 | async-start | bytes 4456448 | tf_op jit(solution)/shard_map/all_gather | solution.py:105
  27.2 430.9 %all-reduce.2.cloned.1.call-start = ((), (), s32[]{:S(2)}) async-start(), calls=%async_computation.4 | async-start | bytes 8388608 | tf_op jit(solution)/shard_map/psum | solution.py:214
  114.4 6.4 %copy-start.2 = (bf16[1024,2048]{1,0:T(8,128)(2,1)S(1)}, bf16[1024,2048]{1,0:T(8,128)(2,1)}, u32[]{:S(2)}) copy-start(bf16[1024,2048]{1,0:T(8,128)(2,1)} %all-gather.4.cloned.1.call-done) | copy-start | bytes 12582916
  121.8 4.1 copy-start.8
  128.4 3.2 copy-start.4
  128.4 3.2 copy-start.16
  128.4 3.2 copy-start.20
  131.6 9.4 %copy-start.17 = (bf16[1024,160]{0,1:T(8,128)(2,1)}, bf16[1024,160]{0,1:T(8,128)(2,1)S(1)}, u32[]{:S(2)}) copy-start(bf16[1024,160]{0,1:T(8,128)(2,1)S(1)} %fusion.49) | copy-start | bytes 983044
  131.6 8.0 %copy-start.18 = (bf16[64,128]{1,0:T(8,128)(2,1)S(1)}, bf16[64,128]{1,0:T(8,128)(2,1)}, u32[]{:S(2)}) copy-start(bf16[64,128]{1,0:T(8,128)(2,1)} %param.31) | copy-start | bytes 49156
  131.6 8.0 %copy-start.19 = (f32[128]{0:T(128)S(1)}, f32[128]{0:T(128)}, u32[]{:S(2)}) copy-start(f32[128]{0:T(128)} %param.32) | copy-start | bytes 1540
  141.0 7.7 %slice-start = ((s8[8388608]{0:T(1024)(128)(4,1)}), s8[4194304]{0:T(1024)(128)(4,1)S(1)}, s32[]{:S(2)}) async-start(s8[8388608]{0:T(1024)(128)(4,1)} %bitcast.290), calls=%async_computation.7 | async-start | bytes 8388608
  141.0 6.2 copy-start.11
  141.0 7.7 %copy-start.3 = (bf16[1024,2048]{1,0:T(8,128)(2,1)S(1)}, bf16[1024,2048]{1,0:T(8,128)(2,1)}, u32[]{:S(2)}) copy-start(bf16[1024,2048]{1,0:T(8,128)(2,1)} %all-gather.4.cloned.1.call-done) | copy-start | bytes 12582916
  141.0 8.4 %slice-start.1 = ((s8[8388608]{0:T(1024)(128)(4,1)}), s8[4194304]{0:T(1024)(128)(4,1)S(1)}, s32[]{:S(2)}) async-start(s8[8388608]{0:T(1024)(128)(4,1)} %bitcast.290), calls=%async_computation.8 | async-start | bytes 8388608
  149.4 3.4 copy-start.10
  154.4 3.6 copy-start.9
  154.4 5.1 copy-start.21
  227.4 50.7 %copy-start.22 = (f32[128]{0:T(128)S(1)}, f32[128]{0:T(128)}, u32[]{:S(2)}) copy-start(f32[128]{0:T(128)} %param.34) | copy-start | bytes 1540
  229.1 3.7 collective-permute-start
  232.9 5.8 collective-permute-start
  238.8 5.8 collective-permute-start
  244.7 5.8 collective-permute-start
  250.6 5.8 collective-permute-start
  256.5 7.4 %collective-permute-start = (bf16[2,64,64]{2,1,0:T(8,128)(2,1)S(1)}, bf16[2,64,64]{2,1,0:T(8,128)(2,1)S(1)}, u32[]{:S(2)}, u32[]{:S(2)}) collective-permute-start(bf16[2,64,64]{2,1,0:T(8,128)(2,1)S(1)} %fusion.135), channel_id=1, source_target_pairs={{0,16},{16,32},{32,48},{48,64},{64,80},{80,96},{96,112},{1,17},{17... | collective-permute-start | bytes 49160 | tf_op jit(solution)/shard_map/while/body/eval_jaxpr/ppermute | solution.py:18
  264.0 7.9 %collective-permute-start = (bf16[2,64,64]{2,1,0:T(8,128)(2,1)S(1)}, bf16[2,64,64]{2,1,0:T(8,128)(2,1)S(1)}, u32[]{:S(2)}, u32[]{:S(2)}) collective-permute-start(bf16[2,64,64]{2,1,0:T(8,128)(2,1)S(1)} %fusion.135), channel_id=1, source_target_pairs={{0,16},{16,32},{32,48},{48,64},{64,80},{80,96},{96,112},{1,17},{17... | collective-permute-start | bytes 49160 | tf_op jit(solution)/shard_map/while/body/eval_jaxpr/ppermute | solution.py:18
  285.9 3.2 copy-start.14
  289.1 16.4 %copy-start.15 = (f32[256,448]{0,1:T(8,128)S(1)}, f32[256,448]{0,1:T(8,128)}, u32[]{:S(2)}) copy-start(f32[256,448]{0,1:T(8,128)} %param.24) | copy-start | bytes 1376260
  290.5 32.3 %all-to-all-start = ((bf16[8,448,256]{2,1,0:T(8,128)(2,1)}), bf16[8,448,256]{2,1,0:T(8,128)(2,1)S(1)}, u32[]{:S(2)}, u32[]{:S(2)}) async-start(bf16[8,448,256]{2,1,0:T(8,128)(2,1)} %stack.4), calls=%async_computation | async-start | bytes 3670016 | tf_op jit(solution)/shard_map/all_to_all | solution.py:117
  305.4 197.8 %all-gather.8.cloned.1.call-start = ((), (), s32[]{:S(2)}) async-start(), calls=%async_computation.5 | async-start | bytes 2064384 | tf_op jit(solution)/shard_map/all_gather | solution.py:114
  306.2 298.2 %reduce-scatter.4.cloned.1.call-start = ((), (), s32[]{:S(2)}) async-start(), calls=%async_computation.6 | async-start | bytes 4456448
  462.8 5.8 copy-start.5
  464.1 7.8 %collective-permute-start.1 = (bf16[1,2048]{1,0:T(2,128)(2,1)S(1)}, bf16[1,2048]{1,0:T(2,128)(2,1)S(1)}, u32[]{:S(2)}, u32[]{:S(2)}) collective-permute-start(bf16[1,2048]{1,0:T(2,128)(2,1)S(1)} %constant_dynamic-slice_fusion.5), channel_id=1, source_target_pairs={{0,16},{16,32},{32,48},{48,64},{64,80},{80,96},{96,112},{1,17},{17... | collective-permute-start | bytes 12296 | tf_op jit(solution)/shard_map/ppermute | solution.py:18
  468.6 3.2 copy-start.7
  474.6 4.7 copy-start.6
  479.3 24.0 %copy-start.12 = (bf16[8,56,8,256]{3,2,0,1:T(8,128)(2,1)S(1)}, bf16[8,56,8,256]{3,2,0,1:T(8,128)(2,1)}, u32[]{:S(2)}) copy-start(bf16[8,56,8,256]{3,2,0,1:T(8,128)(2,1)} %copy.138) | copy-start | bytes 5505028
  515.0 8.2 %copy-start.13 = (f32[8,2,64,64]{3,2,1,0:T(8,128)S(1)}, f32[8,2,64,64]{3,2,1,0:T(8,128)}, u32[]{:S(2)}) copy-start(f32[8,2,64,64]{3,2,1,0:T(8,128)} %get-tuple-element.108) | copy-start | bytes 786436
  604.4 8.5 %copy-start.1 = (bf16[2048,160]{0,1:T(8,128)(2,1)S(1)}, bf16[2048,160]{0,1:T(8,128)(2,1)}, u32[]{:S(2)}) copy-start(bf16[2048,160]{0,1:T(8,128)(2,1)} %param.28) | copy-start | bytes 1966084
Sparse Core Ops, SparseCore 0:
  9.6 44.0 all-gather.5
  56.5 57.8 all-gather.3
  289.2 168.8 all-reduce.1
  460.1 43.1 all-gather.7
  521.6 82.7 reduce-scatter.3
